TPU v7x, 256 devices: a whole 4x4x8 slice. The times are simulated.
256 devices in a mesh: req: 64 (over z, x, core), kv: 4 (over y).
Axes of the slice: x: 4, y: 4, z: 8, core: 2. Of those that a mesh axis runs over, the one named last changes fastest.
Arguments:
- residual_in: bfloat16 [128, 2560], P('req', 'kv'), may hold values from -8 to 8
- queries: bfloat16 [128, 2560], P('req', 'kv'), may hold values from -480 to 480
- fresh_token_keys: bfloat16 [128, 512], P('req', 'kv'), may hold values from -6 to 6
- fresh_token_values: bfloat16 [128, 512], P('req', 'kv'), may hold values from -6 to 6
- cached_key_slots: bfloat16 [128, 4096, 512], P('req', None, 'kv'), may hold values from -6 to 6
- cached_value_slots: bfloat16 [128, 4096, 512], P('req', None, 'kv'), may hold values from -6 to 6
- lengths: int32 [128], replicated, may hold values from 1 to 4096, as said below
- slot_order: int32 [128], replicated, may hold values from 0 to 127, as said below
- out_proj: bfloat16 [2560, 2560], P('kv'), may hold values from -0.5 to 0.5
- norm_gain: bfloat16 [2560], P('kv'), may hold values from 0.5 to 1.5
- expert_ids: int32 [128, 6], replicated, may hold values from 0 to 63, all different within a row; in each aligned block of 128 rows (0 to 127, 128 to 255, ...) at most 24 rows name the same one
- gate_values: float32 [128, 6], replicated, may hold values from 0.1 to 0.5
- gate_proj: bfloat16 [64, 2560, 1536], P('req', None, 'kv'), may hold values from -0.125 to 0.125
- up_proj: bfloat16 [64, 2560, 1536], P('req', None, 'kv'), may hold values from -0.125 to 0.125
- down_proj: bfloat16 [64, 1536, 2560], P('req', 'kv'), may hold values from -0.15625 to 0.15625
Outputs:
- layer_out: bfloat16 [128, 2560], P('req', 'kv')
Inputs may be any that keep to these rules, and one draw needn't show every extreme that they name: `lengths`: each request's count of cached positions; some request has exactly 4096. A permutation of the requests: slot s serves request slot_order[s], and cached_key_slots[s], cached_value_slots[s] hold that request's cache. Requests sorted by decreasing length are dealt to the 64 groups of 2 consecutive slots, one round forward, the next backward. `expert_ids`: each token names 6 different experts; no expert is named by more than 24 tokens, a bound that some block reaches.
All inputs are finite; a program needn't handle non-finite values.
Results may differ from a plain program's by a relative error of at most 0.012.
Values may be sent and summed in bfloat16 or wider, within the bound.
No kernel may reach another device: no remote copies, remote signals or barrier semaphores. Data moves between devices by JAX's collectives and lax.ppermute only.
A program may use at most 64 MiB of HBM per device.

v0:
```python
import math
import jax
import jax.numpy as jnp
from jax import lax
from jax.sharding import PartitionSpec as P

COMBINE = "a2a"


def per_device(
    residual_in,
    queries,
    fresh_token_keys,
    fresh_token_values,
    cached_key_slots,
    cached_value_slots,
    lengths,
    slot_order,
    out_proj,
    norm_gain,
    expert_ids,
    gate_values,
    gate_proj,
    up_proj,
    down_proj,
):
    req_count = lax.axis_size("req")
    kv_count = lax.axis_size("kv")
    req_index = lax.axis_index("req")
    kv_index = lax.axis_index("kv")
    per_dev = residual_in.shape[0]
    head_dim = fresh_token_keys.shape[1]
    col_count = residual_in.shape[1]
    total_reqs = lengths.shape[0]
    model_width = out_proj.shape[1]
    q_width = queries.shape[1]
    packed = jnp.concatenate([queries, fresh_token_keys, fresh_token_values, residual_in], axis=1)
    all_packed = lax.all_gather(packed, "req", axis=0, tiled=True)
    served = lax.dynamic_slice_in_dim(slot_order, req_index * per_dev, per_dev)
    mine = all_packed[served]
    query_rows = mine[:, :q_width].reshape(per_dev, -1, head_dim)
    self_key_row = mine[:, q_width : q_width + head_dim]
    self_value_row = mine[:, q_width + head_dim : q_width + 2 * head_dim]
    residual_rows = mine[:, q_width + 2 * head_dim :]
    live_len = lengths[served]
    inv_root = 1.0 / math.sqrt(head_dim)
    scores = (
        jnp.einsum("rqd,rld->rql", query_rows, cached_key_slots, preferred_element_type=jnp.float32)
        * inv_root
    )
    positions = jnp.arange(cached_key_slots.shape[1])
    scores = jnp.where((positions[None, :] < live_len[:, None])[:, None, :], scores, -1e30)
    own_score = (
        jnp.einsum("rqd,rd->rq", query_rows, self_key_row, preferred_element_type=jnp.float32)
        * inv_root
    )
    highest = jnp.maximum(jnp.max(scores, axis=2), own_score)
    weights = jnp.exp(scores - highest[:, :, None])
    own_weight = jnp.exp(own_score - highest)
    totals = jnp.sum(weights, axis=2) + own_weight
    numerator = jnp.einsum(
        "rql,rld->rqd",
        weights.astype(jnp.bfloat16),
        cached_value_slots,
        preferred_element_type=jnp.float32,
    )
    own_low = lax.optimization_barrier(own_weight.astype(jnp.bfloat16)).astype(jnp.float32)
    numerator = numerator + own_low[:, :, None] * self_value_row.astype(jnp.float32)[:, None, :]
    attended = (numerator / totals[:, :, None]).astype(jnp.bfloat16).reshape(per_dev, -1)
    projected = jnp.dot(attended, out_proj, preferred_element_type=jnp.float32)
    col_start = kv_index * col_count
    own_cols = jnp.concatenate(
        [residual_rows.astype(jnp.float32), norm_gain.astype(jnp.float32)[None, :]], axis=0
    )
    summed_in = jnp.concatenate(
        [projected, jnp.zeros((1, model_width), jnp.float32)], axis=0
    ) + lax.dynamic_update_slice(
        jnp.zeros((per_dev + 1, model_width), jnp.float32), own_cols, (0, col_start)
    )
    summed = lax.psum(summed_in, "kv")
    hidden = summed[:per_dev]
    gain = summed[per_dev]
    squares = jnp.sum(hidden * hidden, axis=1)
    normed = (hidden * lax.rsqrt(squares / model_width + 1e-06)[:, None] * gain).astype(
        jnp.bfloat16
    )
    by_slot = lax.all_gather(normed, "req", axis=0, tiled=True)
    slot_of = (
        jnp.zeros((total_reqs,), jnp.int32)
        .at[slot_order]
        .set(jnp.arange(total_reqs, dtype=jnp.int32))
    )
    local_count = gate_proj.shape[0]
    capacity = min(2 * total_reqs * expert_ids.shape[1] // (local_count * req_count), total_reqs)
    expert = req_index * local_count + 0
    named_here = expert_ids == expert
    token_gate = jnp.sum(jnp.where(named_here, gate_values, 0.0), axis=1)
    uses_expert = jnp.any(named_here, axis=1)
    picked = jnp.nonzero(uses_expert, size=capacity, fill_value=0)[0].astype(jnp.int32)
    valid_rows = jnp.arange(capacity) < jnp.sum(uses_expert.astype(jnp.int32))
    row_block = by_slot[slot_of[picked]]
    gate_h = jnp.dot(row_block, gate_proj[0], preferred_element_type=jnp.float32)
    up_h = jnp.dot(row_block, up_proj[0], preferred_element_type=jnp.float32)
    inner_act = (jax.nn.silu(gate_h) * up_h).astype(jnp.bfloat16)
    outputs = jnp.dot(inner_act, down_proj[0], preferred_element_type=jnp.float32)
    row_gate = jnp.where(valid_rows, token_gate[picked], 0.0)
    weighted = outputs * row_gate[:, None]
    weighted = lax.psum_scatter(weighted, "kv", scatter_dimension=1, tiled=True)
    own_hidden = lax.dynamic_slice_in_dim(hidden, col_start, col_count, axis=1)
    combined = (
        jnp.zeros((total_reqs, col_count), jnp.float32)
        .at[picked]
        .add(weighted)
        .at[served]
        .add(own_hidden)
    )
    if COMBINE == "rs":
        layer_rows = lax.psum_scatter(combined, "req", scatter_dimension=0, tiled=True)
    else:
        layer_rows = jnp.sum(
            lax.all_to_all(
                combined.reshape(req_count, per_dev, col_count), "req", 0, 0, tiled=False
            ),
            axis=0,
        )
    return layer_rows.astype(jnp.bfloat16)


def solution(mesh):
    in_specs = (
        P("req", "kv"),
        P("req", "kv"),
        P("req", "kv"),
        P("req", "kv"),
        P("req", None, "kv"),
        P("req", None, "kv"),
        P(),
        P(),
        P("kv", None),
        P("kv"),
        P(),
        P(),
        P("req", None, "kv"),
        P("req", None, "kv"),
        P("req", "kv", None),
    )
    out_specs = P("req", "kv")
    return jax.shard_map(
        per_device, mesh=mesh, in_specs=in_specs, out_specs=out_specs, check_vma=False
    )
```

profile of v0, /device:TPU:1, one launch (start us, length us, event | category | flops | bytes accessed | tf_op | source)
XLA Modules:
  0.0 225.2 jit_solution(8981033612592452208)
XLA Ops:
  6.5 0.9 compare_select_fusion.4
  8.0 0.7 maximum_bitcast_fusion
  8.7 57.9 %all-gather = bf16[64,2,1536]{2,1,0:T(2,128)(2,1)} all-gather(bf16[1,2,1536]{2,1,0:T(2,128)(2,1)S(1)} %maximum_bitcast_fusion), channel_id=1, replica_groups=mesh['req'=64,'kv'=4] {'req'}, dimensions={0}, use_global_device_ids=true | all-gather | bytes 399360 | tf_op jit(solution)/shard_map/all_gather | solution.py:38
  66.6 1.9 reshape.232
  68.5 1.6 gather_fusion.1
  70.2 1.3 gather_fusion
  71.7 2.3 %fusion.51 = (f32[2,5]{1,0:T(2,128)S(1)}, f32[2,5,4096]{2,1,0:T(8,128)S(1)}) fusion(bf16[2,5,128]{2,1,0:T(8,128)(2,1)S(1)} %reshape.151, bf16[2,4096,128]{2,1,0:T(8,128)(2,1)} %param.19, pred[2,4096]{1,0:T(4,128)(4,1)S(1)} %iota_compare_fusion), kind=kOutput, calls=%fused_computation.85 | convolution fusion | flops 10608630 | bytes 2271784 | tf_op jit(solution)/shard_map/rqd,rld->rql/dot_general | solution.py:48
  76.1 2.0 fusion.16
  78.8 13.9 %psum.7 = f32[3,2560]{1,0:T(4,128)S(1)} all-reduce(f32[3,2560]{1,0:T(4,128)S(1)} %add_dynamic-update-slice_fusion), channel_id=1, replica_groups=mesh['req'=64,'kv'=4] {'kv'}, use_global_device_ids=true, to_apply=%region_7.8 | all-reduce | flops 7680 | bytes 61440 | tf_op jit(solution)/shard_map/psum | solution.py:80
  93.6 56.6 %all-gather.1 = bf16[64,2,2560]{2,1,0:T(2,128)(2,1)} all-gather(bf16[1,2,2560]{2,1,0:T(2,128)(2,1)S(1)} %fusion.34), channel_id=1, replica_groups=mesh['req'=64,'kv'=4] {'req'}, dimensions={0}, use_global_device_ids=true | all-gather | bytes 665600 | tf_op jit(solution)/shard_map/all_gather | solution.py:87
  150.2 2.7 %reshape.234 = bf16[128,2560]{1,0:T(8,128)(2,1)} reshape(bf16[64,2,2560]{2,1,0:T(2,128)(2,1)} %all-gather.1) | data formatting | bytes 1310720
  153.3 1.4 scatter_custom_fusion
  154.9 0.8 fusion.32
  155.6 1.0 scatter_custom_fusion.1
  157.5 0.7 gather_fusion.4
  158.9 1.9 gather_fusion.3
  160.8 1.9 fusion.4
  162.8 3.8 %convolution_multiply_fusion.1 = f32[24,2560]{1,0:T(8,128)} fusion(bf16[1,384,2560]{2,1,0:T(8,128)(2,1)} %param.29, bf16[24,2560]{1,0:T(8,128)(2,1)S(1)} %gather_fusion.3, bf16[1,2560,384]{2,1,0:T(8,128)(2,1)} %param.28, f32[24]{0:T(128)S(1)} %compare_select_fusion.5, f32[24,384]{1,0:T(8,128)S(1)} %fusion.4), kind=kOutput, calls=%fused_computation.11 | convolution fusion | flops 94488576 | bytes 4337760 | tf_op jit(solution)/shard_map/dot_general | solution.py:105
  166.5 16.9 %reduce-scatter.2.cloned.1.call-done = f32[24,640]{1,0:T(8,128)} async-done(((f32[24,2560]{1,0:T(8,128)}), f32[24,640]{1,0:T(8,128)}) %reduce-scatter.2.cloned.1.call-update) | async-done | bytes 61456 | tf_op jit(solution)/shard_map/reduce_scatter | solution.py:108
  183.5 1.7 scatter_custom_fusion.2
  185.2 2.4 %scatter_custom_fusion.3 = f32[128,640]{1,0:T(8,128)} fusion(f32[128,640]{1,0:T(8,128)} %scatter_custom_fusion.2, s32[2]{0:T(128)} %copy-done.3, f32[2,2560]{1,0:T(2,128)S(1)} %get-tuple-element.7, s32[]{:T(128)} %constant.31.clone.1, s32[]{:T(128)S(6)} %select_n.104), kind=kCustom, calls=%fused_computation.54 | custom fusion | flops 1280 | bytes 333316 | tf_op jit(solution)/shard_map/scatter-add | solution.py:115
  187.6 1.9 reshape.153
  189.5 27.2 %all_to_all.5 = f32[64,2,640]{2,1,0:T(2,128)} all-to-all(f32[64,2,640]{2,1,0:T(2,128)} %reshape.153), channel_id=1, replica_groups=mesh['req'=64,'kv'=4] {'req'}, dimensions={0} | all-to-all | bytes 655360 | tf_op jit(solution)/shard_map/all_to_all | solution.py:121
  216.7 1.7 reduce_sum.53
  (47 shorter events, 6.5 us)
Async XLA Ops:
  6.5 71.6 %copy-start = (bf16[640,2560]{1,0:T(8,128)(2,1)S(1)}, bf16[640,2560]{1,0:T(8,128)(2,1)}, u32[]{:S(2)}) copy-start(bf16[640,2560]{1,0:T(8,128)(2,1)} %param.23) | copy-start | bytes 9830404
  6.5 176.9 %reduce-scatter.2.cloned.1.call-start = ((), (), s32[]{:S(2)}) async-start(), calls=%async_computation.2 | async-start | bytes 307200 | tf_op jit(solution)/shard_map/reduce_scatter | solution.py:108
  7.4 0.5 copy-start.3
  78.1 14.7 %copy-start.1 = (f32[128,6]{0,1:T(8,128)S(1)}, f32[128,6]{0,1:T(8,128)}, u32[]{:S(2)}) copy-start(f32[128,6]{0,1:T(8,128)} %param.26) | copy-start | bytes 9220
  78.1 14.7 %copy-start.2 = (s32[128,6]{0,1:T(8,128)S(1)}, s32[128,6]{0,1:T(8,128)}, u32[]{:S(2)}) copy-start(s32[128,6]{0,1:T(8,128)} %param.25) | copy-start | bytes 9220
  78.2 14.7 %copy-start.4 = (s32[128]{0:T(128)S(1)}, s32[128]{0:T(128)}, u32[]{:S(2)}) copy-start(s32[128]{0:T(128)} %param.22) | copy-start | bytes 1540
Sparse Core Ops, SparseCore 0:
  166.7 16.7 reduce-scatter.1
where the time goes:
time: 226 us; the launch traced here: 225 us
  blocking collectives  156 us (69%)
  waiting for transfers between devices  17 us (8%)
  local copies, waits for them, and re-layouts  15.3 us (7%)
  between operations  13.6 us (6%)
  other arithmetic  13.1 us (6%)
  matrix products  10.7 us (5%)
    all_gather x1, blocking collectives, per_device(): all_packed = lax.all_gather(packed, 'req', axis=0, tiled=True)  57.9 us
    all_gather x1, blocking collectives, per_device(): by_slot = lax.all_gather(normed, 'req', axis=0, tiled=True)  56.6 us
    all_to_all x1, blocking collectives, per_device(): lax.all_to_all(combined.reshape(req_count, per_dev, col_count), 'req', 0,...  27.2 us
    reduce_scatter x1, waiting for transfers between devices, per_device(): weighted = lax.psum_scatter(weighted, 'kv', scatter_dimension=1, tiled=True)  16.9 us
    psum x1, blocking collectives, per_device(): summed = lax.psum(summed_in, 'kv')  13.9 us
    unnamed x12, local copies, waits for them, and re-layouts  5.18 us
  transfers between devices with their start and end apart: 1, of which 1 were waited for; matrix products, arithmetic and copies ran while one was open for 0% of the time, Pallas kernels for 0%

commit v1 on v0

--- a/solution.py
+++ b/solution.py
@@ -84,7 +84,9 @@
     normed = (hidden * lax.rsqrt(squares / model_width + 1e-06)[:, None] * gain).astype(
         jnp.bfloat16
     )
-    by_slot = lax.all_gather(normed, "req", axis=0, tiled=True)
+    by_slot = jnp.concatenate(
+        lax.all_to_all(jnp.stack([normed] * lax.axis_size("req")), "req", 0, 0), axis=0
+    )
     slot_of = (
         jnp.zeros((total_reqs,), jnp.int32)
         .at[slot_order]

time: 226 us -> 193 us (0.85)
  blocking collectives: 156 us -> 99 us
  waiting for transfers between devices: 17 us -> 29.6 us
  starting transfers between devices: 0.01 us -> 9.83 us
    all_gather x1 -> x0, blocking collectives: 56.6 us -> none  [per_device(): by_slot = lax.all_gather(normed, 'req', axis=0, tiled=True)]
    all_to_all x0 -> x1, waiting for transfers between devices: none -> 13.5 us  [per_device(): lax.all_to_all(jnp.stack([normed] * lax.axis_size('req')), 'req', 0, 0)]
    all_to_all x0 -> x1, starting transfers between devices: none -> 9.79 us  [per_device(): lax.all_to_all(jnp.stack([normed] * lax.axis_size('req')), 'req', 0, 0)]
    unnamed x12 -> x11, local copies, waits for them, and re-layouts: 5.18 us -> 2.46 us
    reshape x0 -> x1, local copies, waits for them, and re-layouts: none -> 2.71 us  [per_device(): jnp.concatenate(lax.all_to_all(jnp.stack([normed] * lax.axis_size('req'))...]
  transfers between devices with their start and end apart: 1 -> 2, of which waited for: 1 -> 2; matrix products, arithmetic and copies ran while one was open for 0% -> 3% of each run, Pallas kernels for 0% -> 0%
where the time goes in v1:
time: 193 us; the launch traced here: 192 us
  blocking collectives  99 us (51%)
  waiting for transfers between devices  29.6 us (15%)
  local copies, waits for them, and re-layouts  16.5 us (9%)
  between operations  13.6 us (7%)
  other arithmetic  13.1 us (7%)
  matrix products  10.7 us (6%)
  starting transfers between devices  9.83 us (5%)
    all_gather x1, blocking collectives, per_device(): all_packed = lax.all_gather(packed, 'req', axis=0, tiled=True)  57.9 us
    all_to_all x1, blocking collectives, per_device(): lax.all_to_all(combined.reshape(req_count, per_dev, col_count), 'req', 0,...  27.2 us
    reduce_scatter x1, waiting for transfers between devices, per_device(): weighted = lax.psum_scatter(weighted, 'kv', scatter_dimension=1, tiled=True)  16.1 us
    psum x1, blocking collectives, per_device(): summed = lax.psum(summed_in, 'kv')  13.9 us
    all_to_all x1, waiting for transfers between devices, per_device(): lax.all_to_all(jnp.stack([normed] * lax.axis_size('req')), 'req', 0, 0)  13.5 us
    all_to_all x1, starting transfers between devices, per_device(): lax.all_to_all(jnp.stack([normed] * lax.axis_size('req')), 'req', 0, 0)  9.79 us
    scatter-add x2, other arithmetic, per_device(): combined = jnp.zeros((total_reqs, col_count), jnp.float32).at[picked].add...  4.1 us
  transfers between devices with their start and end apart: 2, of which 2 were waited for; matrix products, arithmetic and copies ran while one was open for 3% of the time, Pallas kernels for 0%

profile of v1, /device:TPU:1, one launch (start us, length us, event | category | flops | bytes accessed | tf_op | source)
XLA Modules:
  0.0 192.3 jit_solution(15898165780690832009)
XLA Ops:
  6.5 0.9 compare_select_fusion.4
  8.7 57.9 %all-gather = bf16[64,2,1536]{2,1,0:T(2,128)(2,1)} all-gather(bf16[1,2,1536]{2,1,0:T(2,128)(2,1)S(1)} %maximum_bitcast_fusion), channel_id=1, replica_groups=mesh['req'=64,'kv'=4] {'req'}, dimensions={0}, use_global_device_ids=true | all-gather | bytes 399360 | tf_op jit(solution)/shard_map/all_gather | solution.py:38
  66.6 1.9 reshape.238
  68.5 1.6 gather_fusion.1
  70.2 1.3 gather_fusion
  71.7 2.3 %fusion.50 = (f32[2,5]{1,0:T(2,128)S(1)}, f32[2,5,4096]{2,1,0:T(8,128)S(1)}) fusion(bf16[2,5,128]{2,1,0:T(8,128)(2,1)S(1)} %reshape.156, bf16[2,4096,128]{2,1,0:T(8,128)(2,1)} %param.19, pred[2,4096]{1,0:T(4,128)(4,1)S(1)} %iota_compare_fusion), kind=kOutput, calls=%fused_computation.84 | convolution fusion | flops 10608630 | bytes 2271784 | tf_op jit(solution)/shard_map/rqd,rld->rql/dot_general | solution.py:48
  76.1 2.0 %fusion.16 = bf16[1,2,5,128]{3,2,1,0:T(8,128)(2,1)S(1)} fusion(bf16[2,4096,128]{2,1,0:T(8,128)(2,1)} %param.20, f32[2,5,4096]{2,1,0:T(8,128)S(1)} %get-tuple-element.16, f32[2,5]{1,0:T(2,128)S(1)} %multiply_maximum_fusion, f32[2,5]{1,0:T(2,128)} %get-tuple-element.14, f32[2,128]{1,0:T(2,128)S(1)} %get-tuple-element.11, f32[2,5]{1,0:T(2,128)} %convert_element_type.49), kind=kOutput, calls=%fused_computation.22 | convolution fusion | flops 10572800 | bytes 2264696 | tf_op jit(solution)/shard_map/rql,rld->rqd/dot_general | solution.py:61
  78.7 13.9 %psum.7 = f32[3,2560]{1,0:T(4,128)S(1)} all-reduce(f32[3,2560]{1,0:T(4,128)S(1)} %add_dynamic-update-slice_fusion), channel_id=1, replica_groups=mesh['req'=64,'kv'=4] {'kv'}, use_global_device_ids=true, to_apply=%region_7.8 | all-reduce | flops 7680 | bytes 61440 | tf_op jit(solution)/shard_map/psum | solution.py:80
  92.9 1.2 stack.2
  94.1 9.8 %all-to-all-start = ((bf16[64,2,2560]{2,1,0:T(2,128)(2,1)}), bf16[64,2,2560]{2,1,0:T(2,128)(2,1)}, u32[]{:S(2)}, u32[]{:S(2)}) async-start(bf16[64,2,2560]{2,1,0:T(2,128)(2,1)} %stack.2), calls=%async_computation | async-start | bytes 1310720 | tf_op jit(solution)/shard_map/all_to_all | solution.py:88
  104.4 1.4 scatter_custom_fusion
  106.6 1.0 scatter_custom_fusion.1
  107.6 0.8 fusion.32
  110.6 13.5 %all-to-all-done = bf16[64,2,2560]{2,1,0:T(2,128)(2,1)} async-done(((bf16[64,2,2560]{2,1,0:T(2,128)(2,1)}), bf16[64,2,2560]{2,1,0:T(2,128)(2,1)}, u32[]{:S(2)}, u32[]{:S(2)}) %all-to-all-start) | async-done | bytes 655392 | tf_op jit(solution)/shard_map/all_to_all | solution.py:88
  124.2 2.7 %reshape.158 = bf16[128,2560]{1,0:T(8,128)(2,1)} reshape(bf16[64,2,2560]{2,1,0:T(2,128)(2,1)} %all-to-all-done) | data formatting | bytes 1310720 | tf_op jit(solution)/shard_map/reshape | solution.py:87
  126.9 1.9 gather_fusion.3
  128.8 1.9 %fusion.4 = f32[24,384]{1,0:T(8,128)S(1)} fusion(bf16[24,2560]{1,0:T(8,128)(2,1)S(1)} %gather_fusion.3, bf16[1,2560,384]{2,1,0:T(8,128)(2,1)} %param.27), kind=kOutput, calls=%fused_computation.15 | convolution fusion | flops 47185920 | bytes 2125824 | tf_op jit(solution)/shard_map/dot_general | solution.py:104
  130.7 3.8 %convolution_multiply_fusion.1 = f32[24,2560]{1,0:T(8,128)} fusion(bf16[1,384,2560]{2,1,0:T(8,128)(2,1)} %param.29, bf16[24,2560]{1,0:T(8,128)(2,1)S(1)} %gather_fusion.3, bf16[1,2560,384]{2,1,0:T(8,128)(2,1)} %param.28, f32[24]{0:T(128)S(1)} %compare_select_fusion.5, f32[24,384]{1,0:T(8,128)S(1)} %fusion.4), kind=kOutput, calls=%fused_computation.11 | convolution fusion | flops 94488576 | bytes 4337760 | tf_op jit(solution)/shard_map/dot_general | solution.py:107
  134.5 16.1 %reduce-scatter.2.cloned.1.call-done = f32[24,640]{1,0:T(8,128)} async-done(((f32[24,2560]{1,0:T(8,128)}), f32[24,640]{1,0:T(8,128)}) %reduce-scatter.2.cloned.1.call-update) | async-done | bytes 61456 | tf_op jit(solution)/shard_map/reduce_scatter | solution.py:110
  150.6 1.7 scatter_custom_fusion.2
  152.3 2.4 %scatter_custom_fusion.3 = f32[128,640]{1,0:T(8,128)} fusion(f32[128,640]{1,0:T(8,128)} %scatter_custom_fusion.2, s32[2]{0:T(128)} %copy-done.3, f32[2,2560]{1,0:T(2,128)S(1)} %get-tuple-element.7, s32[]{:T(128)} %constant.31.clone.1, s32[]{:T(128)S(6)} %select_n.104), kind=kCustom, calls=%fused_computation.53 | custom fusion | flops 1280 | bytes 333316 | tf_op jit(solution)/shard_map/scatter-add | solution.py:117
  154.7 1.9 reshape.159
  156.6 27.2 %all_to_all.10 = f32[64,2,640]{2,1,0:T(2,128)} all-to-all(f32[64,2,640]{2,1,0:T(2,128)} %reshape.159), channel_id=1, replica_groups=mesh['req'=64,'kv'=4] {'req'}, dimensions={0} | all-to-all | bytes 655360 | tf_op jit(solution)/shard_map/all_to_all | solution.py:123
  183.8 1.7 reduce_sum.53
  (49 shorter events, 8.0 us)
Async XLA Ops:
  6.5 71.6 %copy-start = (bf16[640,2560]{1,0:T(8,128)(2,1)S(1)}, bf16[640,2560]{1,0:T(8,128)(2,1)}, u32[]{:S(2)}) copy-start(bf16[640,2560]{1,0:T(8,128)(2,1)} %param.23) | copy-start | bytes 9830404
  7.4 0.5 copy-start.3
  78.1 25.8 %copy-start.1 = (f32[128,6]{0,1:T(8,128)S(1)}, f32[128,6]{0,1:T(8,128)}, u32[]{:S(2)}) copy-start(f32[128,6]{0,1:T(8,128)} %param.26) | copy-start | bytes 9220
  78.1 25.8 %copy-start.2 = (s32[128,6]{0,1:T(8,128)S(1)}, s32[128,6]{0,1:T(8,128)}, u32[]{:S(2)}) copy-start(s32[128,6]{0,1:T(8,128)} %param.25) | copy-start | bytes 9220
  78.7 27.3 %copy-start.4 = (s32[128]{0:T(128)S(1)}, s32[128]{0:T(128)}, u32[]{:S(2)}) copy-start(s32[128]{0:T(128)} %param.22) | copy-start | bytes 1540
  94.1 30.1 %all-to-all-start = ((bf16[64,2,2560]{2,1,0:T(2,128)(2,1)}), bf16[64,2,2560]{2,1,0:T(2,128)(2,1)}, u32[]{:S(2)}, u32[]{:S(2)}) async-start(bf16[64,2,2560]{2,1,0:T(2,128)(2,1)} %stack.2), calls=%async_computation | async-start | bytes 1310720 | tf_op jit(solution)/shard_map/all_to_all | solution.py:88
  103.9 46.7 %reduce-scatter.2.cloned.1.call-start = ((), (), s32[]{:S(2)}) async-start(), calls=%async_computation.3 | async-start | bytes 307200 | tf_op jit(solution)/shard_map/reduce_scatter | solution.py:110
Sparse Core Ops, SparseCore 0:
  134.6 15.9 reduce-scatter.1
